TPU v7x, 128 devices: a whole 4x4x4 slice. The times are simulated.
128 devices in a mesh: req: 16 (over y, z), mlp: 8 (over x, core).
Axes of the slice: x: 4, y: 4, z: 4, core: 2. Of those that a mesh axis runs over, the one named last changes fastest.
Arguments:
- resid: bfloat16 [2176, 5120], P('req', 'mlp'), may hold values from -180 to 180
- queries: bfloat16 [2176, 5120], P('req', 'mlp'), may hold values from -200 to 200
- new_keys: bfloat16 [2176, 1024], P('req', 'mlp'), may hold values from -6 to 6
- new_values: bfloat16 [2176, 1024], P('req', 'mlp'), may hold values from -6 to 6
- cache_keys: bfloat16 [48, 4096, 1024], P('req', None, 'mlp'), may hold values from -6 to 6
- cache_values: bfloat16 [48, 4096, 1024], P('req', None, 'mlp'), may hold values from -6 to 6
- context_keys: bfloat16 [5, 1024, 1024], P(None, 'req', 'mlp'), may hold values from -6 to 6
- context_values: bfloat16 [5, 1024, 1024], P(None, 'req', 'mlp'), may hold values from -6 to 6
- cache_lengths: int32 [48], P('req'), may hold values from 1 to 4096, 49152 in all
- group_ids: int32 [48], P('req'), may hold values from 0 to 3
- prefix_lengths: int32 [4], replicated, may hold values from 1 to 1024, 2048 in all
- prompt_start: int32 [1], replicated, may hold values from 1 to 1023
- out_weight: bfloat16 [5120, 5120], P('mlp'), may hold values from -1.25 to 1.25
- norm_gain: float32 [5120], P('mlp'), may hold values from 0.5 to 1.5
- gate_weight: bfloat16 [5120, 27648], P(None, ('req', 'mlp')), may hold values from -0.078125 to 0.078125
- up_weight: bfloat16 [5120, 27648], P(None, ('req', 'mlp')), may hold values from -0.078125 to 0.078125
- down_weight: bfloat16 [27648, 5120], P('req', 'mlp'), may hold values from -0.109375 to 0.109375
Outputs:
- out: bfloat16 [2176, 5120], P('req', 'mlp')
Inputs may be any that keep to these rules, and one draw needn't show every extreme that they name: `cache_lengths`: one decode request has 4096 valid positions. `prefix_lengths`: one group's prompt has 1024 positions.
All inputs are finite; a program needn't handle non-finite values. No bound on the sum of `cache_lengths` on one device may be relied on, other than what follows from the above.
Results may differ from a plain program's by a relative error of at most 0.019.
Values may be sent and summed in bfloat16 or wider, within the bound.
No kernel may reach another device: no remote copies, remote signals or barrier semaphores. Data moves between devices by JAX's collectives and lax.ppermute only.
A program may use at most 128 MiB of HBM per device.

v0:
```python
import math
import jax
import jax.numpy as jnp
from jax import lax
from jax.sharding import PartitionSpec as P

D = 5120
HQ = 40
KV = 8
HD = 128
NEGATIVE = -1e30


def absorb(carried, scores, allowed, values, pattern):
    running, totals, summed = carried
    scores = jnp.where(allowed, scores, -jnp.inf)
    highest = jnp.maximum(running, jnp.max(scores, axis=-1))
    exponent = jnp.where(allowed, jnp.exp(scores - highest[..., None]), 0.0)
    fading = jnp.exp(running - highest)
    weights = exponent.astype(jnp.bfloat16)
    summed = summed * fading[..., None] + jnp.einsum(
        pattern, weights, values, preferred_element_type=jnp.float32
    )
    totals = totals * fading + jnp.sum(exponent, axis=-1)
    return (highest, totals, summed)


def per_device(
    resid,
    queries,
    new_keys,
    new_values,
    cache_keys,
    cache_values,
    context_keys,
    context_values,
    cache_lengths,
    group_ids,
    prefix_lengths,
    prompt_start,
    out_weight,
    norm_gain,
    gate_weight,
    up_weight,
    down_weight,
):
    rows_here = queries.shape[0]
    decode_count = cache_keys.shape[0]
    prompt_count = rows_here - decode_count
    heads_kv = new_keys.shape[1] // HD
    group_size = HQ // KV
    scaling = 1.0 / math.sqrt(HD)
    cache_span = cache_keys.shape[1]
    context_count = context_keys.shape[0]
    query_rows = queries.reshape(rows_here, heads_kv, group_size, HD)
    query_decode = query_rows[:decode_count]
    query_prompt = query_rows[decode_count:]
    key_rows = new_keys.reshape(rows_here, heads_kv, HD)
    value_rows = new_values.reshape(rows_here, heads_kv, HD)

    def fresh_state(row_count):
        return (
            jnp.full((row_count, heads_kv, group_size), NEGATIVE, jnp.float32),
            jnp.zeros((row_count, heads_kv, group_size), jnp.float32),
            jnp.zeros((row_count, heads_kv, group_size, HD), jnp.float32),
        )

    past_keys = cache_keys.reshape(decode_count, cache_span, heads_kv, HD)
    past_values = cache_values.reshape(decode_count, cache_span, heads_kv, HD)
    scores = (
        jnp.einsum("ikgd,ickd->ikgc", query_decode, past_keys, preferred_element_type=jnp.float32)
        * scaling
    )
    usable = (jnp.arange(cache_span)[None, :] < cache_lengths[:, None])[:, None, None, :]
    decode_state = absorb(fresh_state(decode_count), scores, usable, past_values, "ikgc,ickd->ikgd")
    own_scores = (
        jnp.einsum(
            "ikgd,ikd->ikg",
            query_decode,
            key_rows[:decode_count],
            preferred_element_type=jnp.float32,
        )[..., None]
        * scaling
    )
    decode_state = absorb(
        decode_state,
        own_scores,
        jnp.ones(own_scores.shape, dtype=bool),
        value_rows[:decode_count][:, None],
        "ikgc,ickd->ikgd",
    )
    prompt_length = prompt_start[0]
    prefix_here = prefix_lengths[group_ids]
    state_decode = decode_state
    state_prompt = fresh_state(prompt_count)
    req_count = lax.axis_size("req")
    context_rows = context_keys.shape[1]
    packed = jnp.concatenate(
        [
            context_keys.reshape(context_count * context_rows, heads_kv * HD),
            context_values.reshape(context_count * context_rows, heads_kv * HD),
            new_keys,
            new_values,
        ],
        0,
    )
    gathered = lax.all_gather(packed, "req", axis=0, tiled=False)
    context_span = context_count * context_rows

    def context_of(offset):
        piece = gathered[:, offset : offset + context_span]
        piece = piece.reshape(req_count, context_count, context_rows, heads_kv * HD)
        return jnp.transpose(piece, (1, 0, 2, 3)).reshape(
            context_count, req_count * context_rows, heads_kv * HD
        )

    def prompt_of(offset):
        piece = gathered[:, offset : offset + rows_here][:, decode_count:]
        return piece.reshape(req_count * prompt_count, heads_kv * HD)

    key_block = context_of(0)
    value_block = context_of(context_span)
    extent = key_block.shape[1]
    positions = jnp.arange(extent)
    key_split = key_block.reshape(context_count, extent, heads_kv, HD)
    value_split = value_block.reshape(context_count, extent, heads_kv, HD)
    chosen_keys = key_split[group_ids]
    chosen_values = value_split[group_ids]
    block_scores = (
        jnp.einsum("ikgd,ickd->ikgc", query_decode, chosen_keys, preferred_element_type=jnp.float32)
        * scaling
    )
    block_usable = (positions[None, :] < prefix_here[:, None])[:, None, None, :]
    state_decode = absorb(
        state_decode, block_scores, block_usable, chosen_values, "ikgc,ickd->ikgd"
    )
    block_scores = (
        jnp.einsum(
            "jkgd,ckd->jkgc",
            query_prompt,
            key_split[context_count - 1],
            preferred_element_type=jnp.float32,
        )
        * scaling
    )
    block_usable = (positions < prompt_length)[None, None, None, :]
    state_prompt = absorb(
        state_prompt, block_scores, block_usable, value_split[context_count - 1], "jkgc,ckd->jkgd"
    )
    prompt_state = state_prompt
    own_positions = lax.axis_index("req") * prompt_count + jnp.arange(prompt_count, dtype=jnp.int32)
    key_block = prompt_of(2 * context_span)
    value_block = prompt_of(2 * context_span + rows_here)
    extent = key_block.shape[0]
    positions = jnp.arange(extent, dtype=jnp.int32)
    block_scores = (
        jnp.einsum(
            "jkgd,ckd->jkgc",
            query_prompt,
            key_block.reshape(extent, heads_kv, HD),
            preferred_element_type=jnp.float32,
        )
        * scaling
    )
    block_usable = (positions[None, :] <= own_positions[:, None])[:, None, None, :]
    prompt_state = absorb(
        prompt_state,
        block_scores,
        block_usable,
        value_block.reshape(extent, heads_kv, HD),
        "jkgc,ckd->jkgd",
    )

    def finish(carried):
        return (carried[2] / carried[1][..., None]).astype(jnp.bfloat16)

    attended = jnp.concatenate([finish(state_decode), finish(prompt_state)], 0).reshape(
        rows_here, heads_kv * group_size * HD
    )
    mlp_count = lax.axis_size("mlp")
    head_partial = jnp.dot(attended, out_weight, preferred_element_type=jnp.float32)
    pieces = lax.all_to_all(head_partial.astype(jnp.bfloat16), "mlp", 1, 0, tiled=True)
    projected = jnp.sum(pieces.reshape(mlp_count, rows_here, -1).astype(jnp.float32), axis=0)
    mixed = (resid.astype(jnp.float32) + projected).astype(jnp.bfloat16)
    mixed_wide = mixed.astype(jnp.float32)
    gain_pieces = []
    remainder = norm_gain
    for _ in range(3):
        piece = remainder.astype(jnp.bfloat16)
        gain_pieces.append(piece)
        remainder = remainder - piece.astype(jnp.float32)
    with_gain = jnp.concatenate([mixed, jnp.stack(gain_pieces, 0)], 0)
    gathered_rows = lax.all_gather(with_gain, "mlp", axis=1, tiled=True).astype(jnp.float32)
    mixed_rows = gathered_rows[:rows_here]
    full_gain = (
        gathered_rows[rows_here] + gathered_rows[rows_here + 1] + gathered_rows[rows_here + 2]
    )
    square_total = jnp.sum(mixed_rows * mixed_rows, axis=1)
    half = D // 2
    side = lax.axis_index("mlp") % 2
    own_half = lax.dynamic_slice_in_dim(mixed_rows, side * half, half, axis=1)
    own_gain = lax.dynamic_slice_in_dim(full_gain, side * half, half, axis=0)
    normed = (own_half * lax.rsqrt(square_total / D + 1e-06)[:, None] * own_gain[None, :]).astype(
        jnp.bfloat16
    )
    pairs = [(i, i ^ 1) for i in range(mlp_count)]

    def halves(weight):
        return (
            lax.dynamic_slice_in_dim(weight, side * half, half, axis=0),
            lax.dynamic_slice_in_dim(weight, (1 - side) * half, half, axis=0),
        )

    gate_near, gate_far = halves(gate_weight)
    up_near, up_far = halves(up_weight)
    chunk_count = 2
    chunk_rows = rows_here // chunk_count
    feeds = []
    for chunk in range(chunk_count):
        rows = normed[chunk * chunk_rows : (chunk + 1) * chunk_rows]
        near_rows = lax.all_gather(rows, "req", axis=0, tiled=True)
        far_rows = lax.ppermute(near_rows, "mlp", pairs)
        gate_proj = jnp.dot(near_rows, gate_near, preferred_element_type=jnp.float32) + jnp.dot(
            far_rows, gate_far, preferred_element_type=jnp.float32
        )
        up_proj = jnp.dot(near_rows, up_near, preferred_element_type=jnp.float32) + jnp.dot(
            far_rows, up_far, preferred_element_type=jnp.float32
        )
        hidden = (jax.nn.silu(gate_proj) * up_proj).astype(jnp.bfloat16)
        hidden_block = lax.all_gather(hidden, "mlp", axis=1, tiled=True)
        down_partial = jnp.dot(hidden_block, down_weight, preferred_element_type=jnp.float32)
        req_pieces = lax.all_to_all(down_partial.astype(jnp.bfloat16), "req", 0, 0, tiled=True)
        feeds.append(
            jnp.sum(req_pieces.reshape(req_count, chunk_rows, -1).astype(jnp.float32), axis=0)
        )
    feed = jnp.concatenate(feeds, 0)
    return (mixed_wide + feed).astype(jnp.bfloat16)


def solution(mesh):
    return jax.shard_map(
        per_device,
        mesh=mesh,
        in_specs=(
            P("req", "mlp"),
            P("req", "mlp"),
            P("req", "mlp"),
            P("req", "mlp"),
            P("req", None, "mlp"),
            P("req", None, "mlp"),
            P(None, "req", "mlp"),
            P(None, "req", "mlp"),
            P("req"),
            P("req"),
            P(),
            P(),
            P("mlp", None),
            P("mlp"),
            P(None, ("req", "mlp")),
            P(None, ("req", "mlp")),
            P("req", "mlp"),
        ),
        out_specs=P("req", "mlp"),
        check_vma=False,
    )
```

profile of v0, /device:TPU:0, one launch (start us, length us, event | category | flops | bytes accessed | tf_op | source)
XLA Modules:
  0.0 399.9 jit_solution(140865241295268066)
XLA Ops:
  6.5 1.8 pad_maximum_fusion
  8.4 0.7 slice.58
  9.1 1.0 slice.64
  10.1 0.9 reshape.390
  11.6 0.7 compare_select_fusion.1
  12.3 0.6 pad_clamp_fusion
  12.9 1.3 gather_fusion
  14.8 0.7 slice_bitcast_fusion.2
  15.5 1.3 slice_convert_fusion
  16.7 0.7 iota_compare_fusion.2
  17.4 0.7 fusion.98
  18.1 0.7 iota_compare_fusion.1
  18.9 2.3 fusion.114
  21.4 40.6 %all-gather.16.cloned.1.call-done = bf16[14592,128]{1,0:T(8,128)(2,1)} async-done(((bf16[912,128]{1,0:T(8,128)(2,1)}), bf16[14592,128]{1,0:T(8,128)(2,1)}) %all-gather.16.cloned.1.call-update) | async-done | bytes 3735568 | tf_op jit(solution)/shard_map/all_gather | solution.py:107
  62.0 1.9 fusion.110
  63.9 2.6 fusion.109
  66.5 1.2 copy.26
  67.7 0.7 slice.82
  68.4 1.2 copy.27
  69.6 0.7 slice.83
  70.4 1.7 gather_fusion.1
  72.0 2.1 gather_fusion.2
  74.2 1.6 fusion.115
  76.6 2.5 fusion.45
  79.3 1.0 reshape.441
  80.3 1.3 fusion.113
  81.7 0.7 bitcast_reduce_fusion
  82.3 1.4 fusion
  83.8 0.8 fusion.15
  84.8 0.8 fusion.34
  85.8 1.4 fusion.52
  87.4 0.7 slice-done.1
  88.1 1.3 convolution_convert_fusion
  89.4 1.2 copy.75
  90.6 4.4 %all-to-all-start = ((bf16[136,8,640]{2,0,1:T(8,128)(2,1)}), bf16[136,8,640]{2,0,1:T(8,128)(2,1)S(1)}, u32[]{:S(2)}, u32[]{:S(2)}) async-start(bf16[136,8,640]{2,0,1:T(8,128)(2,1)} %bitcast.172), calls=%async_computation | async-start | bytes 2785280 | tf_op jit(solution)/shard_map/all_to_all | solution.py:182
  95.3 19.3 %all-to-all-done = bf16[136,8,640]{2,0,1:T(8,128)(2,1)S(1)} async-done(((bf16[136,8,640]{2,0,1:T(8,128)(2,1)}), bf16[136,8,640]{2,0,1:T(8,128)(2,1)S(1)}, u32[]{:S(2)}, u32[]{:S(2)}) %all-to-all-start) | async-done | bytes 1392672 | tf_op jit(solution)/shard_map/all_to_all | solution.py:182
  114.8 0.7 pad_maximum_fusion.1
  115.6 21.5 %all-gather.10.cloned.1.call-done = bf16[139,5120]{1,0:T(8,128)(2,1)} async-done(((bf16[139,640]{1,0:T(8,128)(2,1)}), bf16[139,5120]{1,0:T(8,128)(2,1)}) %all-gather.10.cloned.1.call-update) | async-done | bytes 1423376 | tf_op jit(solution)/shard_map/all_gather | solution.py:193
  137.2 1.8 convert_element_type.97
  139.8 0.9 slice_bitcast_fusion.1
  141.4 59.1 %all-gather.18.cloned.1.call-done = bf16[16,68,2560]{2,1,0:T(8,128)(2,1)} async-done(((bf16[1,68,2560]{2,1,0:T(8,128)(2,1)}), bf16[16,68,2560]{2,1,0:T(8,128)(2,1)}) %all-gather.18.cloned.1.call-update) | async-done | bytes 5570576 | tf_op jit(solution)/shard_map/all_gather | solution.py:221
  200.5 7.9 %reshape.433 = bf16[1088,2560]{1,0:T(8,128)(2,1)} reshape(bf16[16,68,2560]{2,1,0:T(8,128)(2,1)} %all-gather.18.cloned.1.call-done) | data formatting | bytes 11141120
  208.4 53.3 %all-gather.20.cloned.1.call-done = bf16[16,68,2560]{2,1,0:T(8,128)(2,1)} async-done(((bf16[1,68,2560]{2,1,0:T(8,128)(2,1)}), bf16[16,68,2560]{2,1,0:T(8,128)(2,1)}) %all-gather.20.cloned.1.call-update) | async-done | bytes 5570576 | tf_op jit(solution)/shard_map/all_gather | solution.py:221
  261.7 7.9 %reshape.435 = bf16[1088,2560]{1,0:T(8,128)(2,1)} reshape(bf16[16,68,2560]{2,1,0:T(8,128)(2,1)} %all-gather.20.cloned.1.call-done) | data formatting | bytes 11141120
  269.6 4.7 %fusion.65 = f32[1088,216]{0,1:T(8,128)S(1)} fusion(bf16[1088,2560]{1,0:T(8,128)(2,1)} %reshape.433, bf16[5120,216]{0,1:T(8,128)(2,1)S(1)} %copy-done.21, s32[]{:T(128)S(6)} %select_n.78), kind=kOutput, calls=%fused_computation.72 | convolution fusion | flops 1203240960 | bytes 7616516 | tf_op jit(solution)/shard_map/dot_general | solution.py:223
  274.5 2.0 fusion.59
  276.5 4.6 %convolution_add_fusion.3 = f32[1088,216]{0,1:T(8,128)S(1)} fusion(f32[1088,216]{0,1:T(8,128)S(1)} %fusion.65, bf16[1088,2560]{1,0:T(8,128)(2,1)} %collective-permute-done, bf16[5120,216]{0,1:T(8,128)(2,1)S(1)} %copy-done.21, s32[]{:T(128)S(6)} %select_n.79), kind=kOutput, calls=%fused_computation.31 | convolution fusion | flops 1203475968 | bytes 8611844 | tf_op jit(solution)/shard_map/dot_general | solution.py:223
  281.1 5.5 %fusion.13 = bf16[1088,216]{0,1:T(8,128)(2,1)} fusion(f32[1088,216]{0,1:T(8,128)S(1)} %fusion.59, bf16[1088,2560]{1,0:T(8,128)(2,1)} %collective-permute-done, f32[1088,216]{0,1:T(8,128)S(1)} %convolution_add_fusion.3, bf16[5120,216]{0,1:T(8,128)(2,1)S(1)} %copy-done.22, s32[]{:T(128)S(6)} %select_n.79), kind=kOutput, calls=%fused_computation.32 | convolution fusion | flops 1204886016 | bytes 9137156 | tf_op jit(solution)/shard_map/dot_general | solution.py:226
  286.9 4.7 %fusion.63 = f32[1088,216]{0,1:T(8,128)S(1)} fusion(bf16[1088,2560]{1,0:T(8,128)(2,1)} %reshape.435, bf16[5120,216]{0,1:T(8,128)(2,1)S(1)} %copy-done.21, s32[]{:T(128)S(6)} %select_n.78), kind=kOutput, calls=%fused_computation.70 | convolution fusion | flops 1203240960 | bytes 7616516 | tf_op jit(solution)/shard_map/dot_general | solution.py:223
  291.6 4.6 %fusion.57 = f32[1088,216]{0,1:T(8,128)S(1)} fusion(bf16[1088,2560]{1,0:T(8,128)(2,1)} %reshape.435, bf16[5120,216]{0,1:T(8,128)(2,1)S(1)} %copy-done.23, s32[]{:T(128)S(6)} %select_n.78), kind=kOutput, calls=%fused_computation.64 | convolution fusion | flops 1203240960 | bytes 7616516 | tf_op jit(solution)/shard_map/dot_general | solution.py:226
  296.2 4.9 %convolution_add_fusion.1 = f32[1088,216]{0,1:T(8,128)S(1)} fusion(f32[1088,216]{0,1:T(8,128)S(1)} %fusion.63, bf16[1088,2560]{1,0:T(8,128)(2,1)} %collective-permute-done.1, bf16[5120,216]{0,1:T(8,128)(2,1)S(1)} %copy-done.21, s32[]{:T(128)S(6)} %select_n.79), kind=kOutput, calls=%fused_computation.28 | convolution fusion | flops 1203475968 | bytes 8611844 | tf_op jit(solution)/shard_map/dot_general | solution.py:223
  301.2 5.5 %fusion.14 = bf16[1088,216]{0,1:T(8,128)(2,1)} fusion(f32[1088,216]{0,1:T(8,128)S(1)} %fusion.57, bf16[1088,2560]{1,0:T(8,128)(2,1)} %collective-permute-done.1, f32[1088,216]{0,1:T(8,128)S(1)} %convolution_add_fusion.1, bf16[5120,216]{0,1:T(8,128)(2,1)S(1)} %copy-done.23, s32[]{:T(128)S(6)} %select_n.79), kind=kOutput, calls=%fused_computation.33 | convolution fusion | flops 1204886016 | bytes 9137156 | tf_op jit(solution)/shard_map/dot_general | solution.py:226
  306.7 10.9 %all-gather.12.cloned.1.call-done = bf16[1088,1728]{0,1:T(8,128)(2,1)} async-done(((bf16[1088,216]{0,1:T(8,128)(2,1)}), bf16[1088,1728]{0,1:T(8,128)(2,1)}) %all-gather.12.cloned.1.call-update) | async-done | bytes 3760144 | tf_op jit(solution)/shard_map/all_gather | solution.py:230
  317.6 6.1 %convolution_convert_fusion.2 = bf16[1088,640]{1,0:T(8,128)(2,1)S(1)} fusion(bf16[1088,1728]{0,1:T(8,128)(2,1)} %all-gather.12.cloned.1.call-done, bf16[1728,640]{1,0:T(8,128)(2,1)} %param.33), kind=kOutput, calls=%fused_computation.11 | convolution fusion | flops 2407178240 | bytes 7364608 | tf_op jit(solution)/shard_map/dot_general | solution.py:231
  323.7 1.3 all_to_all.24
  325.0 7.2 %all-to-all-start.1 = ((bf16[16,68,640]{2,1,0:T(8,128)(2,1)}), bf16[16,68,640]{2,1,0:T(8,128)(2,1)}, u32[]{:S(2)}, u32[]{:S(2)}) async-start(bf16[16,68,640]{2,1,0:T(8,128)(2,1)} %all_to_all.24), calls=%async_computation.1 | async-start | bytes 2949120 | tf_op jit(solution)/shard_map/all_to_all | solution.py:232
  332.2 18.1 %all-gather.14.cloned.1.call-done = bf16[1088,1728]{0,1:T(8,128)(2,1)} async-done(((bf16[1088,216]{0,1:T(8,128)(2,1)}), bf16[1088,1728]{0,1:T(8,128)(2,1)}) %all-gather.14.cloned.1.call-update) | async-done | bytes 3760144 | tf_op jit(solution)/shard_map/all_gather | solution.py:230
  350.3 6.6 %convolution_convert_fusion.1 = bf16[1088,640]{1,0:T(8,128)(2,1)} fusion(bf16[1088,1728]{0,1:T(8,128)(2,1)} %all-gather.14.cloned.1.call-done, bf16[1728,640]{1,0:T(8,128)(2,1)S(1)} %copy-done.24), kind=kOutput, calls=%fused_computation.10 | convolution fusion | flops 2407178240 | bytes 7364608 | tf_op jit(solution)/shard_map/dot_general | solution.py:231
  356.9 3.4 all_to_all.26
  360.3 7.0 %all-to-all-start.2 = ((bf16[16,68,640]{2,1,0:T(8,128)(2,1)}), bf16[16,68,640]{2,1,0:T(8,128)(2,1)}, u32[]{:S(2)}, u32[]{:S(2)}) async-start(bf16[16,68,640]{2,1,0:T(8,128)(2,1)} %all_to_all.26), calls=%async_computation.2 | async-start | bytes 2949120 | tf_op jit(solution)/shard_map/all_to_all | solution.py:232
  367.3 1.6 convert_reduce_fusion.1
  368.9 21.8 %all-to-all-done.2 = bf16[16,68,640]{2,1,0:T(8,128)(2,1)} async-done(((bf16[16,68,640]{2,1,0:T(8,128)(2,1)}), bf16[16,68,640]{2,1,0:T(8,128)(2,1)}, u32[]{:S(2)}, u32[]{:S(2)}) %all-to-all-start.2) | async-done | bytes 1392672 | tf_op jit(solution)/shard_map/all_to_all | solution.py:232
  390.7 1.6 convert_reduce_fusion
  392.3 0.7 fusion.67
  (99 shorter events, 4.9 us)
Async XLA Ops:
  6.5 12.3 %copy-start = (bf16[3,4096,128]{2,1,0:T(8,128)(2,1)S(1)}, bf16[3,4096,128]{2,1,0:T(8,128)(2,1)}, u32[]{:S(2)}) copy-start(bf16[3,4096,128]{2,1,0:T(8,128)(2,1)} %param.21) | copy-start | bytes 9437188
  6.5 55.5 %all-gather.16.cloned.1.call-start = ((), (), s32[]{:S(2)}) async-start(), calls=%async_computation.6 | async-start | bytes 3969024 | tf_op jit(solution)/shard_map/all_gather | solution.py:107
  10.1 8.0 %copy-start.14 = (bf16[3,5,128]{2,1,0:T(8,128)(2,1)}, bf16[3,5,128]{2,1,0:T(8,128)(2,1)S(1)}, u32[]{:S(2)}) copy-start(bf16[3,5,128]{2,1,0:T(8,128)(2,1)S(1)} %reshape.382) | copy-start | bytes 11524
  68.4 1.9 copy-start.4
  68.4 5.7 %copy-start.13 = (pred[3,1024]{1,0:T(4,128)(4,1)S(1)}, pred[3,1024]{1,0:T(4,128)(4,1)}, u32[]{:S(2)}) copy-start(pred[3,1024]{1,0:T(4,128)(4,1)} %iota_compare_fusion.2) | copy-start | bytes 9220
  68.4 5.8 %copy-start.15 = (bf16[3,5,128]{2,1,0:T(8,128)(2,1)S(1)}, bf16[3,5,128]{2,1,0:T(8,128)(2,1)}, u32[]{:S(2)}) copy-start(bf16[3,5,128]{2,1,0:T(8,128)(2,1)} %copy-done.14) | copy-start | bytes 11524
  69.6 6.2 %copy-start.16 = (f32[3,5]{1,0:T(4,128)S(1)}, f32[3,5]{1,0:T(4,128)}, u32[]{:S(2)}) copy-start(f32[3,5]{1,0:T(4,128)} %get-tuple-element.34) | copy-start | bytes 184
  69.6 6.2 %copy-start.19 = (f32[3,1,5]{2,1,0:T(1,128)S(1)}, f32[3,1,5]{2,1,0:T(1,128)}, u32[]{:S(2)}) copy-start(f32[3,1,5]{2,1,0:T(1,128)} %fusion.98) | copy-start | bytes 184
  70.4 6.2 %copy-start.18 = (f32[3,128]{1,0:T(4,128)S(1)}, f32[3,128]{1,0:T(4,128)}, u32[]{:S(2)}) copy-start(f32[3,128]{1,0:T(4,128)} %slice_convert_fusion) | copy-start | bytes 4612
  74.2 4.9 %copy-start.6 = (bf16[16,133,128]{2,1,0:T(8,128)(2,1)S(1)}, bf16[16,133,128]{2,1,0:T(8,128)(2,1)}, u32[]{:S(2)}) copy-start(bf16[16,133,128]{2,1,0:T(8,128)(2,1)} %get-tuple-element.8) | copy-start | bytes 1634308
  76.3 3.0 copy-start.5
  76.6 3.7 copy-start.7
  80.3 1.3 copy-start.8
  80.3 1.4 copy-start.9
  80.3 1.4 copy-start.17
  83.8 1.0 copy-start.11
  84.8 1.0 copy-start.10
  84.8 2.6 slice-start
  85.8 2.3 slice-start.1
  89.3 5.9 %copy-start.20 = (f32[640]{0:T(1024)S(1)}, f32[640]{0:T(1024)}, u32[]{:S(2)}) copy-start(f32[640]{0:T(1024)} %param.30) | copy-start | bytes 7684
  90.6 24.2 %copy-start.12 = (bf16[136,640]{1,0:T(8,128)(2,1)S(1)}, bf16[136,640]{1,0:T(8,128)(2,1)}, u32[]{:S(2)}) copy-start(bf16[136,640]{1,0:T(8,128)(2,1)} %param.17) | copy-start | bytes 522244
  90.6 24.0 %all-to-all-start = ((bf16[136,8,640]{2,0,1:T(8,128)(2,1)}), bf16[136,8,640]{2,0,1:T(8,128)(2,1)S(1)}, u32[]{:S(2)}, u32[]{:S(2)}) async-start(bf16[136,8,640]{2,0,1:T(8,128)(2,1)} %bitcast.172), calls=%async_computation | async-start | bytes 2785280 | tf_op jit(solution)/shard_map/all_to_all | solution.py:182
  95.0 42.2 %all-gather.10.cloned.1.call-start = ((), (), s32[]{:S(2)}) async-start(), calls=%async_computation.3 | async-start | bytes 1658880 | tf_op jit(solution)/shard_map/all_gather | solution.py:193
  115.6 84.9 %all-gather.18.cloned.1.call-start = ((), (), s32[]{:S(2)}) async-start(), calls=%async_computation.7 | async-start | bytes 6266880 | tf_op jit(solution)/shard_map/all_gather | solution.py:221
  137.1 2.1 copy-start.2
  140.8 120.9 %all-gather.20.cloned.1.call-start = ((), (), s32[]{:S(2)}) async-start(), calls=%async_computation.8 | async-start | bytes 6266880 | tf_op jit(solution)/shard_map/all_gather | solution.py:221
  141.3 176.3 %all-gather.12.cloned.1.call-start = ((), (), s32[]{:S(2)}) async-start(), calls=%async_computation.4 | async-start | bytes 4478976 | tf_op jit(solution)/shard_map/all_gather | solution.py:230
  208.4 68.1 %collective-permute-start = (bf16[1088,2560]{1,0:T(8,128)(2,1)}, bf16[1088,2560]{1,0:T(8,128)(2,1)}, u32[]{:S(2)}, u32[]{:S(2)}) collective-permute-start(bf16[1088,2560]{1,0:T(8,128)(2,1)} %reshape.433), channel_id=1, source_target_pairs={{0,1},{1,0},{2,3},{3,2},{4,5},{5,4},{6,7},{7,6},{8,9},{9,8},{10,11... | collective-permute-start | bytes 16711688 | tf_op jit(solution)/shard_map/ppermute | solution.py:222
  208.4 61.2 %copy-start.21 = (bf16[5120,216]{0,1:T(8,128)(2,1)S(1)}, bf16[5120,216]{0,1:T(8,128)(2,1)}, u32[]{:S(2)}) copy-start(bf16[5120,216]{0,1:T(8,128)(2,1)} %param.31) | copy-start | bytes 6635524
  269.5 4.8 %copy-start.3 = (bf16[1088,2560]{1,0:T(8,128)(2,1)S(1)}, bf16[1088,2560]{1,0:T(8,128)(2,1)}, u32[]{:S(2)}) copy-start(bf16[1088,2560]{1,0:T(8,128)(2,1)} %reshape.433) | copy-start | bytes 16711684
  269.5 4.9 %copy-start.22 = (bf16[5120,216]{0,1:T(8,128)(2,1)S(1)}, bf16[5120,216]{0,1:T(8,128)(2,1)}, u32[]{:S(2)}) copy-start(bf16[5120,216]{0,1:T(8,128)(2,1)} %param.32) | copy-start | bytes 6635524
  269.6 26.7 %collective-permute-start.1 = (bf16[1088,2560]{1,0:T(8,128)(2,1)}, bf16[1088,2560]{1,0:T(8,128)(2,1)}, u32[]{:S(2)}, u32[]{:S(2)}) collective-permute-start(bf16[1088,2560]{1,0:T(8,128)(2,1)} %reshape.435), channel_id=1, source_target_pairs={{0,1},{1,0},{2,3},{3,2},{4,5},{5,4},{6,7},{7,6},{8,9},{9,8},{10,11... | collective-permute-start | bytes 16711688 | tf_op jit(solution)/shard_map/ppermute | solution.py:222
  286.6 63.7 %all-gather.14.cloned.1.call-start = ((), (), s32[]{:S(2)}) async-start(), calls=%async_computation.5 | async-start | bytes 4478976 | tf_op jit(solution)/shard_map/all_gather | solution.py:230
  286.9 4.7 %copy-start.23 = (bf16[5120,216]{0,1:T(8,128)(2,1)S(1)}, bf16[5120,216]{0,1:T(8,128)(2,1)}, u32[]{:S(2)}) copy-start(bf16[5120,216]{0,1:T(8,128)(2,1)} %param.32) | copy-start | bytes 6635524
  325.0 25.3 %copy-start.24 = (bf16[1728,640]{1,0:T(8,128)(2,1)S(1)}, bf16[1728,640]{1,0:T(8,128)(2,1)}, u32[]{:S(2)}) copy-start(bf16[1728,640]{1,0:T(8,128)(2,1)} %param.33) | copy-start | bytes 6635524
  325.0 35.2 %all-to-all-start.1 = ((bf16[16,68,640]{2,1,0:T(8,128)(2,1)}), bf16[16,68,640]{2,1,0:T(8,128)(2,1)}, u32[]{:S(2)}, u32[]{:S(2)}) async-start(bf16[16,68,640]{2,1,0:T(8,128)(2,1)} %all_to_all.24), calls=%async_computation.1 | async-start | bytes 2949120 | tf_op jit(solution)/shard_map/all_to_all | solution.py:232
  356.9 36.1 %copy-start.1 = (bf16[3,4096,128]{2,1,0:T(8,128)(2,1)S(1)}, bf16[3,4096,128]{2,1,0:T(8,128)(2,1)}, u32[]{:S(2)}) copy-start(bf16[3,4096,128]{2,1,0:T(8,128)(2,1)} %param.21) | copy-start | bytes 9437188
  360.3 30.4 %all-to-all-start.2 = ((bf16[16,68,640]{2,1,0:T(8,128)(2,1)}), bf16[16,68,640]{2,1,0:T(8,128)(2,1)}, u32[]{:S(2)}, u32[]{:S(2)}) async-start(bf16[16,68,640]{2,1,0:T(8,128)(2,1)} %all_to_all.26), calls=%async_computation.2 | async-start | bytes 2949120 | tf_op jit(solution)/shard_map/all_to_all | solution.py:232
Sparse Core Ops, SparseCore 0:
  9.5 52.4 all-gather.15
  115.7 21.4 all-gather.9
  140.9 59.5 all-gather.17
  202.5 59.0 all-gather.19
  286.7 30.8 all-gather.11
  319.2 31.0 all-gather.13
where the time goes:
time: 401 us; the launch traced here: 400 us
  waiting for transfers between devices  245 us (61%)
  matrix products  62.1 us (15%)
  local copies, waits for them, and re-layouts  42.2 us (11%)
  starting transfers between devices  19.2 us (5%)
  other arithmetic  16.5 us (4%)
  between operations  14.6 us (4%)
    all_gather x2, waiting for transfers between devices, per_device(): near_rows = lax.all_gather(rows, 'req', axis=0, tiled=True)  112 us
    all_gather x1, waiting for transfers between devices, per_device(): gathered = lax.all_gather(packed, 'req', axis=0, tiled=False)  40.6 us
    all_gather x2, waiting for transfers between devices, per_device(): hidden_block = lax.all_gather(hidden, 'mlp', axis=1, tiled=True)  29 us
    all_to_all x2, waiting for transfers between devices, per_device(): lax.all_to_all(down_partial.astype(jnp.bfloat16), 'req', 0, 0, tiled=True)  21.8 us
    all_gather x1, waiting for transfers between devices, per_device(): lax.all_gather(with_gain, 'mlp', axis=1, tiled=True).astype(jnp.float32)  21.5 us
    all_to_all x1, waiting for transfers between devices, per_device(): lax.all_to_all(head_partial.astype(jnp.bfloat16), 'mlp', 1, 0, tiled=True)  19.3 us
    unnamed x60, local copies, waits for them, and re-layouts  18.1 us
    all_to_all x2, starting transfers between devices, per_device(): lax.all_to_all(down_partial.astype(jnp.bfloat16), 'req', 0, 0, tiled=True)  14.2 us
  transfers between devices with their start and end apart: 11, of which 8 were waited for; matrix products, arithmetic and copies ran while one was open for 20% of the time, Pallas kernels for 0%

commit v1 on v0

--- a/solution.py
+++ b/solution.py
@@ -190,7 +190,9 @@
         gain_pieces.append(piece)
         remainder = remainder - piece.astype(jnp.float32)
     with_gain = jnp.concatenate([mixed, jnp.stack(gain_pieces, 0)], 0)
-    gathered_rows = lax.all_gather(with_gain, "mlp", axis=1, tiled=True).astype(jnp.float32)
+    gathered_rows = jnp.concatenate(
+        lax.all_to_all(jnp.stack([with_gain] * lax.axis_size("mlp")), "mlp", 0, 0), axis=1
+    ).astype(jnp.float32)
     mixed_rows = gathered_rows[:rows_here]
     full_gain = (
         gathered_rows[rows_here] + gathered_rows[rows_here + 1] + gathered_rows[rows_here + 2]

time: 401 us -> 402 us (level)
  starting transfers between devices: 19.2 us -> 23.3 us
    all_gather x1 -> x0, waiting for transfers between devices: 21.5 us -> none  [per_device(): lax.all_gather(with_gain, 'mlp', axis=1, tiled=True).astype(jnp.float32)]
    all_to_all x0 -> x1, waiting for transfers between devices: none -> 20.4 us  [per_device(): lax.all_to_all(jnp.stack([with_gain] * lax.axis_size('mlp')), 'mlp', 0, 0)]
    all_to_all x0 -> x1, starting transfers between devices: none -> 4.28 us  [per_device(): lax.all_to_all(jnp.stack([with_gain] * lax.axis_size('mlp')), 'mlp', 0, 0)]
    unnamed x60 -> x59, local copies, waits for them, and re-layouts: 18.1 us -> 18.3 us
where the time goes in v1:
time: 402 us; the launch traced here: 401 us
  waiting for transfers between devices  242 us (60%)
  matrix products  62.1 us (15%)
  local copies, waits for them, and re-layouts  43.7 us (11%)
  starting transfers between devices  23.3 us (6%)
  other arithmetic  15.6 us (4%)
  between operations  14.3 us (4%)
    all_gather x2, waiting for transfers between devices, per_device(): near_rows = lax.all_gather(rows, 'req', axis=0, tiled=True)  110 us
    all_gather x1, waiting for transfers between devices, per_device(): gathered = lax.all_gather(packed, 'req', axis=0, tiled=False)  40.6 us
    all_gather x2, waiting for transfers between devices, per_device(): hidden_block = lax.all_gather(hidden, 'mlp', axis=1, tiled=True)  29 us
    all_to_all x2, waiting for transfers between devices, per_device(): lax.all_to_all(down_partial.astype(jnp.bfloat16), 'req', 0, 0, tiled=True)  21.8 us
    all_to_all x1, waiting for transfers between devices, per_device(): lax.all_to_all(jnp.stack([with_gain] * lax.axis_size('mlp')), 'mlp', 0, 0)  20.4 us
    all_to_all x1, waiting for transfers between devices, per_device(): lax.all_to_all(head_partial.astype(jnp.bfloat16), 'mlp', 1, 0, tiled=True)  19.6 us
    unnamed x59, local copies, waits for them, and re-layouts  18.3 us
    all_to_all x2, starting transfers between devices, per_device(): lax.all_to_all(down_partial.astype(jnp.bfloat16), 'req', 0, 0, tiled=True)  14.2 us
  transfers between devices with their start and end apart: 11, of which 8 were waited for; matrix products, arithmetic and copies ran while one was open for 20% of the time, Pallas kernels for 0%

profile of v1, /device:TPU:0, one launch (start us, length us, event | category | flops | bytes accessed | tf_op | source)
XLA Modules:
  0.0 400.6 jit_solution(16310610305223102010)
XLA Ops:
  6.5 1.8 pad_maximum_fusion
  8.4 0.7 slice.64
  9.1 1.0 slice.70
  10.1 0.9 reshape.401
  12.9 1.3 gather_fusion
  14.8 0.7 slice_bitcast_fusion.3
  15.5 1.3 slice_convert_fusion
  16.7 0.7 iota_compare_fusion.2
  17.4 0.7 fusion.89
  18.1 0.7 iota_compare_fusion.1
  18.9 2.3 fusion.112
  21.4 40.6 %all-gather.13.cloned.1.call-done = bf16[14592,128]{1,0:T(8,128)(2,1)} async-done(((bf16[912,128]{1,0:T(8,128)(2,1)}), bf16[14592,128]{1,0:T(8,128)(2,1)}) %all-gather.13.cloned.1.call-update) | async-done | bytes 3735568 | tf_op jit(solution)/shard_map/all_gather | solution.py:107
  62.0 1.9 fusion.109
  63.9 2.6 fusion.108
  66.5 1.2 copy.26
  67.7 0.7 slice.89
  68.4 1.2 copy.27
  69.6 0.7 slice.90
  70.4 1.7 gather_fusion.1
  72.0 2.1 gather_fusion.2
  74.2 1.6 fusion.113
  76.6 2.5 fusion.45
  79.3 1.0 reshape.452
  80.3 1.3 fusion.111
  81.7 0.7 bitcast_reduce_fusion
  82.3 1.4 fusion
  83.8 0.8 fusion.15
  84.8 0.8 fusion.34
  85.8 1.4 fusion.52
  87.4 0.7 slice-done.1
  88.1 1.3 convolution_convert_fusion
  89.4 1.2 copy.77
  90.6 4.4 %all-to-all-start = ((bf16[136,8,640]{2,0,1:T(8,128)(2,1)}), bf16[136,8,640]{2,0,1:T(8,128)(2,1)S(1)}, u32[]{:S(2)}, u32[]{:S(2)}) async-start(bf16[136,8,640]{2,0,1:T(8,128)(2,1)} %bitcast.178), calls=%async_computation | async-start | bytes 2785280 | tf_op jit(solution)/shard_map/all_to_all | solution.py:182
  95.0 19.6 %all-to-all-done = bf16[136,8,640]{2,0,1:T(8,128)(2,1)S(1)} async-done(((bf16[136,8,640]{2,0,1:T(8,128)(2,1)}), bf16[136,8,640]{2,0,1:T(8,128)(2,1)S(1)}, u32[]{:S(2)}, u32[]{:S(2)}) %all-to-all-start) | async-done | bytes 1392672 | tf_op jit(solution)/shard_map/all_to_all | solution.py:182
  114.9 1.2 stack.11
  116.1 4.3 %all-to-all-start.1 = ((bf16[8,139,640]{2,1,0:T(8,128)(2,1)}), bf16[8,139,640]{2,1,0:T(8,128)(2,1)}, u32[]{:S(2)}, u32[]{:S(2)}) async-start(bf16[8,139,640]{2,1,0:T(8,128)(2,1)} %stack.11), calls=%async_computation.1 | async-start | bytes 2949120 | tf_op jit(solution)/shard_map/all_to_all | solution.py:194
  120.5 20.4 %all-to-all-done.1 = bf16[8,139,640]{2,1,0:T(8,128)(2,1)} async-done(((bf16[8,139,640]{2,1,0:T(8,128)(2,1)}), bf16[8,139,640]{2,1,0:T(8,128)(2,1)}, u32[]{:S(2)}, u32[]{:S(2)}) %all-to-all-start.1) | async-done | bytes 1423392 | tf_op jit(solution)/shard_map/all_to_all | solution.py:194
  140.9 1.6 convert_bitcast_fusion
  143.6 0.9 slice_bitcast_fusion.2
  144.6 0.7 all-gather.17.cloned.1.call-update
  145.3 56.1 %all-gather.15.cloned.1.call-done = bf16[16,68,2560]{2,1,0:T(8,128)(2,1)} async-done(((bf16[1,68,2560]{2,1,0:T(8,128)(2,1)}), bf16[16,68,2560]{2,1,0:T(8,128)(2,1)}) %all-gather.15.cloned.1.call-update) | async-done | bytes 5570576 | tf_op jit(solution)/shard_map/all_gather | solution.py:223
  201.4 7.9 %reshape.444 = bf16[1088,2560]{1,0:T(8,128)(2,1)} reshape(bf16[16,68,2560]{2,1,0:T(8,128)(2,1)} %all-gather.15.cloned.1.call-done) | data formatting | bytes 11141120
  209.2 53.5 %all-gather.17.cloned.1.call-done = bf16[16,68,2560]{2,1,0:T(8,128)(2,1)} async-done(((bf16[1,68,2560]{2,1,0:T(8,128)(2,1)}), bf16[16,68,2560]{2,1,0:T(8,128)(2,1)}) %all-gather.17.cloned.1.call-update) | async-done | bytes 5570576 | tf_op jit(solution)/shard_map/all_gather | solution.py:223
  262.7 7.9 %reshape.446 = bf16[1088,2560]{1,0:T(8,128)(2,1)} reshape(bf16[16,68,2560]{2,1,0:T(8,128)(2,1)} %all-gather.17.cloned.1.call-done) | data formatting | bytes 11141120
  270.6 4.7 %fusion.65 = f32[1088,216]{0,1:T(8,128)S(1)} fusion(bf16[1088,2560]{1,0:T(8,128)(2,1)} %reshape.444, bf16[5120,216]{0,1:T(8,128)(2,1)S(1)} %copy-done.20, s32[]{:T(128)S(6)} %select_n.78), kind=kOutput, calls=%fused_computation.74 | convolution fusion | flops 1203240960 | bytes 7616516 | tf_op jit(solution)/shard_map/dot_general | solution.py:225
  275.5 2.0 fusion.59
  277.5 4.6 %convolution_add_fusion.3 = f32[1088,216]{0,1:T(8,128)S(1)} fusion(f32[1088,216]{0,1:T(8,128)S(1)} %fusion.65, bf16[1088,2560]{1,0:T(8,128)(2,1)} %collective-permute-done, bf16[5120,216]{0,1:T(8,128)(2,1)S(1)} %copy-done.20, s32[]{:T(128)S(6)} %select_n.79), kind=kOutput, calls=%fused_computation.33 | convolution fusion | flops 1203475968 | bytes 8611844 | tf_op jit(solution)/shard_map/dot_general | solution.py:225
  282.1 5.5 %fusion.13 = bf16[1088,216]{0,1:T(8,128)(2,1)} fusion(f32[1088,216]{0,1:T(8,128)S(1)} %fusion.59, bf16[1088,2560]{1,0:T(8,128)(2,1)} %collective-permute-done, f32[1088,216]{0,1:T(8,128)S(1)} %convolution_add_fusion.3, bf16[5120,216]{0,1:T(8,128)(2,1)S(1)} %copy-done.21, s32[]{:T(128)S(6)} %select_n.79), kind=kOutput, calls=%fused_computation.34 | convolution fusion | flops 1204886016 | bytes 9137156 | tf_op jit(solution)/shard_map/dot_general | solution.py:228
  287.9 4.7 %fusion.63 = f32[1088,216]{0,1:T(8,128)S(1)} fusion(bf16[1088,2560]{1,0:T(8,128)(2,1)} %reshape.446, bf16[5120,216]{0,1:T(8,128)(2,1)S(1)} %copy-done.20, s32[]{:T(128)S(6)} %select_n.78), kind=kOutput, calls=%fused_computation.72 | convolution fusion | flops 1203240960 | bytes 7616516 | tf_op jit(solution)/shard_map/dot_general | solution.py:225
  292.7 4.6 %fusion.57 = f32[1088,216]{0,1:T(8,128)S(1)} fusion(bf16[1088,2560]{1,0:T(8,128)(2,1)} %reshape.446, bf16[5120,216]{0,1:T(8,128)(2,1)S(1)} %copy-done.22, s32[]{:T(128)S(6)} %select_n.78), kind=kOutput, calls=%fused_computation.66 | convolution fusion | flops 1203240960 | bytes 7616516 | tf_op jit(solution)/shard_map/dot_general | solution.py:228
  297.3 5.0 %convolution_add_fusion.1 = f32[1088,216]{0,1:T(8,128)S(1)} fusion(f32[1088,216]{0,1:T(8,128)S(1)} %fusion.63, bf16[1088,2560]{1,0:T(8,128)(2,1)} %collective-permute-done.1, bf16[5120,216]{0,1:T(8,128)(2,1)S(1)} %copy-done.20, s32[]{:T(128)S(6)} %select_n.79), kind=kOutput, calls=%fused_computation.30 | convolution fusion | flops 1203475968 | bytes 8611844 | tf_op jit(solution)/shard_map/dot_general | solution.py:225
  302.2 5.5 %fusion.14 = bf16[1088,216]{0,1:T(8,128)(2,1)} fusion(f32[1088,216]{0,1:T(8,128)S(1)} %fusion.57, bf16[1088,2560]{1,0:T(8,128)(2,1)} %collective-permute-done.1, f32[1088,216]{0,1:T(8,128)S(1)} %convolution_add_fusion.1, bf16[5120,216]{0,1:T(8,128)(2,1)S(1)} %copy-done.22, s32[]{:T(128)S(6)} %select_n.79), kind=kOutput, calls=%fused_computation.35 | convolution fusion | flops 1204886016 | bytes 9137156 | tf_op jit(solution)/shard_map/dot_general | solution.py:228
  307.8 10.9 %all-gather.9.cloned.1.call-done = bf16[1088,1728]{0,1:T(8,128)(2,1)} async-done(((bf16[1088,216]{0,1:T(8,128)(2,1)}), bf16[1088,1728]{0,1:T(8,128)(2,1)}) %all-gather.9.cloned.1.call-update) | async-done | bytes 3760144 | tf_op jit(solution)/shard_map/all_gather | solution.py:232
  318.7 6.1 %convolution_convert_fusion.2 = bf16[1088,640]{1,0:T(8,128)(2,1)S(1)} fusion(bf16[1088,1728]{0,1:T(8,128)(2,1)} %all-gather.9.cloned.1.call-done, bf16[1728,640]{1,0:T(8,128)(2,1)} %param.33), kind=kOutput, calls=%fused_computation.11 | convolution fusion | flops 2407178240 | bytes 7364608 | tf_op jit(solution)/shard_map/dot_general | solution.py:233
  324.8 1.3 all_to_all.28
  326.1 7.2 %all-to-all-start.2 = ((bf16[16,68,640]{2,1,0:T(8,128)(2,1)}), bf16[16,68,640]{2,1,0:T(8,128)(2,1)}, u32[]{:S(2)}, u32[]{:S(2)}) async-start(bf16[16,68,640]{2,1,0:T(8,128)(2,1)} %all_to_all.28), calls=%async_computation.2 | async-start | bytes 2949120 | tf_op jit(solution)/shard_map/all_to_all | solution.py:234
  333.3 18.1 %all-gather.11.cloned.1.call-done = bf16[1088,1728]{0,1:T(8,128)(2,1)} async-done(((bf16[1088,216]{0,1:T(8,128)(2,1)}), bf16[1088,1728]{0,1:T(8,128)(2,1)}) %all-gather.11.cloned.1.call-update) | async-done | bytes 3760144 | tf_op jit(solution)/shard_map/all_gather | solution.py:232
  351.4 6.6 %convolution_convert_fusion.1 = bf16[1088,640]{1,0:T(8,128)(2,1)} fusion(bf16[1088,1728]{0,1:T(8,128)(2,1)} %all-gather.11.cloned.1.call-done, bf16[1728,640]{1,0:T(8,128)(2,1)S(1)} %copy-done.23), kind=kOutput, calls=%fused_computation.10 | convolution fusion | flops 2407178240 | bytes 7364608 | tf_op jit(solution)/shard_map/dot_general | solution.py:233
  357.9 3.4 all_to_all.30
  361.3 7.0 %all-to-all-start.3 = ((bf16[16,68,640]{2,1,0:T(8,128)(2,1)}), bf16[16,68,640]{2,1,0:T(8,128)(2,1)}, u32[]{:S(2)}, u32[]{:S(2)}) async-start(bf16[16,68,640]{2,1,0:T(8,128)(2,1)} %all_to_all.30), calls=%async_computation.3 | async-start | bytes 2949120 | tf_op jit(solution)/shard_map/all_to_all | solution.py:234
  368.4 1.6 convert_reduce_fusion.1
  370.0 21.8 %all-to-all-done.3 = bf16[16,68,640]{2,1,0:T(8,128)(2,1)} async-done(((bf16[16,68,640]{2,1,0:T(8,128)(2,1)}), bf16[16,68,640]{2,1,0:T(8,128)(2,1)}, u32[]{:S(2)}, u32[]{:S(2)}) %all-to-all-start.3) | async-done | bytes 1392672 | tf_op jit(solution)/shard_map/all_to_all | solution.py:234
  391.7 1.6 convert_reduce_fusion
  393.3 0.7 fusion.67
  (98 shorter events, 5.6 us)
Async XLA Ops:
  6.5 12.3 %copy-start = (bf16[3,4096,128]{2,1,0:T(8,128)(2,1)S(1)}, bf16[3,4096,128]{2,1,0:T(8,128)(2,1)}, u32[]{:S(2)}) copy-start(bf16[3,4096,128]{2,1,0:T(8,128)(2,1)} %param.21) | copy-start | bytes 9437188
  6.5 55.5 %all-gather.13.cloned.1.call-start = ((), (), s32[]{:S(2)}) async-start(), calls=%async_computation.6 | async-start | bytes 3969024 | tf_op jit(solution)/shard_map/all_gather | solution.py:107
  10.1 8.0 %copy-start.13 = (bf16[3,5,128]{2,1,0:T(8,128)(2,1)}, bf16[3,5,128]{2,1,0:T(8,128)(2,1)S(1)}, u32[]{:S(2)}) copy-start(bf16[3,5,128]{2,1,0:T(8,128)(2,1)S(1)} %reshape.393) | copy-start | bytes 11524
  68.4 1.9 copy-start.3
  68.4 5.7 %copy-start.12 = (pred[3,1024]{1,0:T(4,128)(4,1)S(1)}, pred[3,1024]{1,0:T(4,128)(4,1)}, u32[]{:S(2)}) copy-start(pred[3,1024]{1,0:T(4,128)(4,1)} %iota_compare_fusion.2) | copy-start | bytes 9220
  68.4 5.8 %copy-start.14 = (bf16[3,5,128]{2,1,0:T(8,128)(2,1)S(1)}, bf16[3,5,128]{2,1,0:T(8,128)(2,1)}, u32[]{:S(2)}) copy-start(bf16[3,5,128]{2,1,0:T(8,128)(2,1)} %copy-done.13) | copy-start | bytes 11524
  69.6 6.2 %copy-start.15 = (f32[3,5]{1,0:T(4,128)S(1)}, f32[3,5]{1,0:T(4,128)}, u32[]{:S(2)}) copy-start(f32[3,5]{1,0:T(4,128)} %get-tuple-element.31) | copy-start | bytes 184
  69.6 6.2 %copy-start.18 = (f32[3,1,5]{2,1,0:T(1,128)S(1)}, f32[3,1,5]{2,1,0:T(1,128)}, u32[]{:S(2)}) copy-start(f32[3,1,5]{2,1,0:T(1,128)} %fusion.89) | copy-start | bytes 184
  70.4 6.2 %copy-start.17 = (f32[3,128]{1,0:T(4,128)S(1)}, f32[3,128]{1,0:T(4,128)}, u32[]{:S(2)}) copy-start(f32[3,128]{1,0:T(4,128)} %slice_convert_fusion) | copy-start | bytes 4612
  74.2 4.9 %copy-start.5 = (bf16[16,133,128]{2,1,0:T(8,128)(2,1)S(1)}, bf16[16,133,128]{2,1,0:T(8,128)(2,1)}, u32[]{:S(2)}) copy-start(bf16[16,133,128]{2,1,0:T(8,128)(2,1)} %get-tuple-element.8) | copy-start | bytes 1634308
  76.3 3.0 copy-start.4
  76.6 3.7 copy-start.6
  80.3 1.3 copy-start.7
  80.3 1.4 copy-start.8
  80.3 1.4 copy-start.16
  83.8 1.0 copy-start.10
  84.8 1.0 copy-start.9
  84.8 2.6 slice-start
  85.8 2.3 slice-start.1
  89.3 5.6 %copy-start.19 = (f32[640]{0:T(1024)S(1)}, f32[640]{0:T(1024)}, u32[]{:S(2)}) copy-start(f32[640]{0:T(1024)} %param.30) | copy-start | bytes 7684
  90.6 24.2 %copy-start.11 = (bf16[136,640]{1,0:T(8,128)(2,1)S(1)}, bf16[136,640]{1,0:T(8,128)(2,1)}, u32[]{:S(2)}) copy-start(bf16[136,640]{1,0:T(8,128)(2,1)} %param.17) | copy-start | bytes 522244
  90.6 24.0 %all-to-all-start = ((bf16[136,8,640]{2,0,1:T(8,128)(2,1)}), bf16[136,8,640]{2,0,1:T(8,128)(2,1)S(1)}, u32[]{:S(2)}, u32[]{:S(2)}) async-start(bf16[136,8,640]{2,0,1:T(8,128)(2,1)} %bitcast.178), calls=%async_computation | async-start | bytes 2785280 | tf_op jit(solution)/shard_map/all_to_all | solution.py:182
  116.1 24.8 %all-to-all-start.1 = ((bf16[8,139,640]{2,1,0:T(8,128)(2,1)}), bf16[8,139,640]{2,1,0:T(8,128)(2,1)}, u32[]{:S(2)}, u32[]{:S(2)}) async-start(bf16[8,139,640]{2,1,0:T(8,128)(2,1)} %stack.11), calls=%async_computation.1 | async-start | bytes 2949120 | tf_op jit(solution)/shard_map/all_to_all | solution.py:194
  120.4 81.0 %all-gather.15.cloned.1.call-start = ((), (), s32[]{:S(2)}) async-start(), calls=%async_computation.7 | async-start | bytes 6266880 | tf_op jit(solution)/shard_map/all_gather | solution.py:223
  144.5 118.2 %all-gather.17.cloned.1.call-start = ((), (), s32[]{:S(2)}) async-start(), calls=%async_computation.8 | async-start | bytes 6266880 | tf_op jit(solution)/shard_map/all_gather | solution.py:223
  145.2 173.4 %all-gather.9.cloned.1.call-start = ((), (), s32[]{:S(2)}) async-start(), calls=%async_computation.4 | async-start | bytes 4478976 | tf_op jit(solution)/shard_map/all_gather | solution.py:232
  209.2 68.2 %collective-permute-start = (bf16[1088,2560]{1,0:T(8,128)(2,1)}, bf16[1088,2560]{1,0:T(8,128)(2,1)}, u32[]{:S(2)}, u32[]{:S(2)}) collective-permute-start(bf16[1088,2560]{1,0:T(8,128)(2,1)} %reshape.444), channel_id=1, source_target_pairs={{0,1},{1,0},{2,3},{3,2},{4,5},{5,4},{6,7},{7,6},{8,9},{9,8},{10,11... | collective-permute-start | bytes 16711688 | tf_op jit(solution)/shard_map/ppermute | solution.py:224
  209.2 61.3 %copy-start.20 = (bf16[5120,216]{0,1:T(8,128)(2,1)S(1)}, bf16[5120,216]{0,1:T(8,128)(2,1)}, u32[]{:S(2)}) copy-start(bf16[5120,216]{0,1:T(8,128)(2,1)} %param.31) | copy-start | bytes 6635524
  270.6 4.7 %copy-start.2 = (bf16[1088,2560]{1,0:T(8,128)(2,1)S(1)}, bf16[1088,2560]{1,0:T(8,128)(2,1)}, u32[]{:S(2)}) copy-start(bf16[1088,2560]{1,0:T(8,128)(2,1)} %reshape.444) | copy-start | bytes 16711684
  270.6 4.9 %copy-start.21 = (bf16[5120,216]{0,1:T(8,128)(2,1)S(1)}, bf16[5120,216]{0,1:T(8,128)(2,1)}, u32[]{:S(2)}) copy-start(bf16[5120,216]{0,1:T(8,128)(2,1)} %param.32) | copy-start | bytes 6635524
  270.6 26.7 %collective-permute-start.1 = (bf16[1088,2560]{1,0:T(8,128)(2,1)}, bf16[1088,2560]{1,0:T(8,128)(2,1)}, u32[]{:S(2)}, u32[]{:S(2)}) collective-permute-start(bf16[1088,2560]{1,0:T(8,128)(2,1)} %reshape.446), channel_id=1, source_target_pairs={{0,1},{1,0},{2,3},{3,2},{4,5},{5,4},{6,7},{7,6},{8,9},{9,8},{10,11... | collective-permute-start | bytes 16711688 | tf_op jit(solution)/shard_map/ppermute | solution.py:224
  287.6 63.7 %all-gather.11.cloned.1.call-start = ((), (), s32[]{:S(2)}) async-start(), calls=%async_computation.5 | async-start | bytes 4478976 | tf_op jit(solution)/shard_map/all_gather | solution.py:232
  287.9 4.7 %copy-start.22 = (bf16[5120,216]{0,1:T(8,128)(2,1)S(1)}, bf16[5120,216]{0,1:T(8,128)(2,1)}, u32[]{:S(2)}) copy-start(bf16[5120,216]{0,1:T(8,128)(2,1)} %param.32) | copy-start | bytes 6635524
  326.1 25.3 %copy-start.23 = (bf16[1728,640]{1,0:T(8,128)(2,1)S(1)}, bf16[1728,640]{1,0:T(8,128)(2,1)}, u32[]{:S(2)}) copy-start(bf16[1728,640]{1,0:T(8,128)(2,1)} %param.33) | copy-start | bytes 6635524
  326.1 35.2 %all-to-all-start.2 = ((bf16[16,68,640]{2,1,0:T(8,128)(2,1)}), bf16[16,68,640]{2,1,0:T(8,128)(2,1)}, u32[]{:S(2)}, u32[]{:S(2)}) async-start(bf16[16,68,640]{2,1,0:T(8,128)(2,1)} %all_to_all.28), calls=%async_computation.2 | async-start | bytes 2949120 | tf_op jit(solution)/shard_map/all_to_all | solution.py:234
  357.9 36.1 %copy-start.1 = (bf16[3,4096,128]{2,1,0:T(8,128)(2,1)S(1)}, bf16[3,4096,128]{2,1,0:T(8,128)(2,1)}, u32[]{:S(2)}) copy-start(bf16[3,4096,128]{2,1,0:T(8,128)(2,1)} %param.21) | copy-start | bytes 9437188
  361.3 30.4 %all-to-all-start.3 = ((bf16[16,68,640]{2,1,0:T(8,128)(2,1)}), bf16[16,68,640]{2,1,0:T(8,128)(2,1)}, u32[]{:S(2)}, u32[]{:S(2)}) async-start(bf16[16,68,640]{2,1,0:T(8,128)(2,1)} %all_to_all.30), calls=%async_computation.3 | async-start | bytes 2949120 | tf_op jit(solution)/shard_map/all_to_all | solution.py:234
Sparse Core Ops, SparseCore 0:
  9.5 52.4 all-gather.12
  144.6 56.7 all-gather.14
  203.6 59.0 all-gather.16
  287.8 30.8 all-gather.8
  320.3 31.0 all-gather.10
